TPU v7x, 32 devices: a whole 2x2x4 slice. The times are simulated.
32 devices in a mesh: section: 2 (over core), dp: 16 (over z, y, x).
Axes of the slice: x: 2, y: 2, z: 4, core: 2. Of those that a mesh axis runs over, the one named last changes fastest.
Arguments:
- acts: bfloat16 [2, 16, 1, 64, 2, 2, 128], P('section', 'dp'), may hold values from -6 to 6
- preacts: bfloat16 [2, 16, 1, 64, 2, 2, 128], P('section', 'dp'), may hold values from -6 to 6
- top_grad: bfloat16 [16, 1, 64, 2, 2, 128], P('dp'), may hold values from -6 to 6
- weights: bfloat16 [2, 64, 1728], P('section'), may hold values from -0.21875 to 0.21875
- a_factor: bfloat16 [2, 1728, 1728], P('section', 'dp'), as said below
- g_factor: bfloat16 [2, 64, 64], P('section'), as said below
Outputs:
- act_grads: bfloat16 [2, 16, 1, 64, 2, 2, 128], P('section', 'dp')
- update: float32 [2, 1728, 64], P('section', 'dp')
- inverse: float32 [2, 1728, 1728], P('section', 'dp')
Inputs may be any that keep to these rules, and one draw needn't show every extreme that they name: `a_factor`: each matrix is symmetric and positive definite. `g_factor`: each matrix is symmetric and positive definite.
All inputs are finite; a program needn't handle non-finite values. Where the computation divides by a largest or mean magnitude, that divisor is 1e-20 or more.
Results may differ from a plain program's by a relative error of at most 0.006.
Values may be sent and summed in bfloat16 or wider, within the bound.
No kernel may reach another device: no remote copies, remote signals or barrier semaphores. Data moves between devices by JAX's collectives and lax.ppermute only.
A program may use at most 64 MiB of HBM per device.

v0:
```python
import jax
import jax.numpy as jnp
from jax import lax
from jax.sharding import PartitionSpec as P

KW = 3
MICRO = 1


def shifted(value, axis, steps):
    count = lax.axis_size(axis)
    first, last = (max(0, -steps), min(count, count - steps))
    return lax.ppermute(value, axis, [(source, source + steps) for source in range(first, last)])


def tap_offsets(kernel_width):
    middle = kernel_width // 2
    result = []
    for along_x in range(kernel_width):
        for along_y in range(kernel_width):
            for along_z in range(kernel_width):
                result.append((along_x - middle, along_y - middle, along_z - middle))
    return result


def taps_stack(volume, kernel_width, direction):
    middle = kernel_width // 2
    padded = jnp.pad(volume, ((0, 0), (middle, middle), (middle, middle), (middle, middle)))
    size_x, size_y, size_z = (volume.shape[1], volume.shape[2], volume.shape[3])
    pieces = []
    for off_x, off_y, off_z in tap_offsets(kernel_width):
        start_x = middle + direction * off_x
        start_y = middle + direction * off_y
        start_z = middle + direction * off_z
        pieces.append(
            padded[
                :,
                start_x : start_x + size_x,
                start_y : start_y + size_y,
                start_z : start_z + size_z,
            ]
        )
    stacked = jnp.stack(pieces, 0)
    return stacked.reshape(len(pieces) * volume.shape[0], size_x * size_y * size_z)


def back_input(grad_out, w_rows):
    columns = taps_stack(grad_out, KW, -1)
    summed = lax.dot_general(
        w_rows, columns, (((0,), (0,)), ((), ())), preferred_element_type=jnp.float32
    )
    return summed.astype(jnp.bfloat16).reshape(grad_out.shape)


def back_weight(volume, grad_out):
    columns = taps_stack(volume, KW, 1)
    flattened = grad_out.reshape(grad_out.shape[0], -1)
    return lax.dot_general(
        columns, flattened, (((1,), (1,)), ((), ())), preferred_element_type=jnp.float32
    )


def local_inverse(matrix):
    values = matrix.astype(jnp.float32)
    step_size = 1.0 / jnp.max(jnp.sum(jnp.abs(values), axis=1))
    identity = jnp.eye(matrix.shape[0], dtype=jnp.float32)
    resid0 = (identity - step_size * values).astype(jnp.bfloat16)
    resid1 = jnp.dot(resid0, resid0, preferred_element_type=jnp.float32).astype(jnp.bfloat16)
    cross_term = jnp.dot(resid1, resid0, preferred_element_type=jnp.float32)
    return step_size * (
        identity + resid0.astype(jnp.float32) + resid1.astype(jnp.float32) + cross_term
    )


def eye_rows(start_row, row_total, order_full):
    column_ids = lax.broadcasted_iota(jnp.int32, (row_total, order_full), 1)
    row_ids = lax.broadcasted_iota(jnp.int32, (row_total, order_full), 0)
    return (column_ids == start_row + row_ids).astype(jnp.float32)


def doubling_sum(value, axis):
    count = lax.axis_size(axis)
    assert count & count - 1 == 0
    stride = 1
    while stride < count:
        value = value + lax.ppermute(value, axis, [(i, i ^ stride) for i in range(count)])
        stride *= 2
    return value


def shards(acts, preacts, top_grad, weights, a_factor, g_factor):
    section_index = lax.axis_index("section")
    section_count = lax.axis_size("section")
    tick_count = MICRO + section_count - 1
    gathered = lax.all_gather(a_factor[0], "dp", axis=0, tiled=True)
    inputs = acts[0, 0]
    pre_values = preacts[0, 0]
    upper_grads = top_grad[0]
    channels = weights.shape[1]
    w_rows = weights[0].reshape(channels, -1, channels).transpose(1, 0, 2).reshape(-1, channels)
    zero_field = jnp.zeros(inputs.shape[1:], jnp.bfloat16)

    def one_tick(tick_index, carried):
        outgoing, stored_grads, stored_slopes = carried
        incoming = shifted(outgoing, "section", -1)
        micro_index = tick_index - (section_count - 1 - section_index)
        is_valid = jnp.logical_and(micro_index >= 0, micro_index < MICRO)
        clipped = jnp.clip(micro_index, 0, MICRO - 1)
        from_top = lax.dynamic_index_in_dim(upper_grads, clipped, 0, keepdims=False)
        arriving = jnp.where(section_index == section_count - 1, from_top, incoming)
        pre_now = lax.dynamic_index_in_dim(pre_values, clipped, 0, keepdims=False)
        grad_out = jnp.where(pre_now > 0, arriving, zero_field)
        sending = back_input(grad_out, w_rows)
        old_grad = lax.dynamic_index_in_dim(stored_grads, clipped, 0, keepdims=False)
        old_slope = lax.dynamic_index_in_dim(stored_slopes, clipped, 0, keepdims=False)
        stored_grads = lax.dynamic_update_index_in_dim(
            stored_grads, jnp.where(is_valid, sending, old_grad), clipped, 0
        )
        stored_slopes = lax.dynamic_update_index_in_dim(
            stored_slopes, jnp.where(is_valid, grad_out, old_slope), clipped, 0
        )
        return (sending, stored_grads, stored_slopes)

    start_state = (
        zero_field,
        jnp.zeros(inputs.shape, jnp.bfloat16),
        jnp.zeros(inputs.shape, jnp.bfloat16),
    )
    last_sent, stored_grads, stored_slopes = lax.fori_loop(0, tick_count, one_tick, start_state)
    local_grad = back_weight(inputs[0], stored_slopes[0])
    summed_grad = doubling_sum(local_grad, "dp")
    mean_grad = summed_grad / lax.axis_size("dp")
    a_rows = a_factor[0]
    row_total = a_rows.shape[0]
    order_full = a_rows.shape[1]
    first_row = lax.axis_index("dp") * row_total
    full_values = gathered.astype(jnp.float32)
    step_size = 1.0 / jnp.max(jnp.sum(jnp.abs(full_values), axis=1))
    full_resid0 = (jnp.eye(order_full, dtype=jnp.float32) - step_size * full_values).astype(
        jnp.bfloat16
    )
    own_eye = eye_rows(first_row, row_total, order_full)
    resid0 = (own_eye - step_size * a_rows.astype(jnp.float32)).astype(jnp.bfloat16)
    resid1 = jnp.dot(resid0, full_resid0, preferred_element_type=jnp.float32).astype(jnp.bfloat16)
    cross_term = jnp.dot(resid1, full_resid0, preferred_element_type=jnp.float32)
    inverse_rows = step_size * (
        own_eye + resid0.astype(jnp.float32) + resid1.astype(jnp.float32) + cross_term
    )
    g_inverse = local_inverse(g_factor[0])
    preconditioned = jnp.dot(
        mean_grad, g_inverse, precision=lax.Precision.HIGHEST, preferred_element_type=jnp.float32
    )
    update_rows = jnp.dot(
        inverse_rows,
        preconditioned,
        precision=lax.Precision.HIGHEST,
        preferred_element_type=jnp.float32,
    )
    return (stored_grads[None, None], update_rows[None], inverse_rows[None])


def solution(mesh):
    placed = (
        P("section", "dp", None, None, None, None, None),
        P("section", "dp", None, None, None, None, None),
        P("dp", None, None, None, None, None),
        P("section", None, None),
        P("section", "dp", None),
        P("section", None, None),
    )
    return jax.shard_map(
        shards,
        mesh=mesh,
        in_specs=placed,
        out_specs=(
            P("section", "dp", None, None, None, None, None),
            P("section", "dp", None),
            P("section", "dp", None),
        ),
        check_vma=False,
    )
```

profile of v0, /device:TPU:7, one launch (start us, length us, event | category | flops | bytes accessed | tf_op | source)
XLA Modules:
  0.0 239.3 jit_solution(13392514546595699222)
XLA Ops:
  7.2 2.5 %copy.17 = bf16[1,108,1728]{2,0,1:T(2,128)(2,1)} copy(bf16[1,108,1728]{2,1,0:T(8,128)(2,1)} %param.12) | data formatting | bytes 746496 | tf_op args[4]
  9.8 0.5 reshape_squeeze.6
  10.3 0.9 copy.19
  12.3 0.2 fusion.85
  12.6 0.2 fusion.89
  12.7 0.2 fusion.91
  13.0 0.2 fusion.93
  13.1 0.2 fusion.95
  13.4 0.2 fusion.99
  13.8 0.1 fusion.105
  14.5 0.1 fusion.117
  14.6 2.3 reshape.66
  16.9 0.7 broadcast.37
  17.5 0.6 broadcast.38
  18.2 24.4 %while.20 = (s32[]{:T(128)}, bf16[64,2,2,128]{3,2,1,0:T(2,128)(2,1)}, bf16[1,64,2,2,128]{4,3,2,1,0:T(2,128)(2,1)}, bf16[1,64,2,2,128]{4,3,2,1,0:T(2,128)(2,1)}, ...) while((s32[]{:T(128)}, ...), condition=%wide.region_1.2_spmd.clone, body=%wide.region_0.1_spmd.clone.sunk | while | flops 113475592 | bytes 10772739 | solution.py:129
  18.2 2.6 %collective-permute-start = (bf16[64,2,2,128]{3,2,1,0:T(2,128)(2,1)}, bf16[64,2,2,128]{3,2,1,0:T(2,128)(2,1)S(1)}, u32[]{:S(2)}, u32[]{:S(2)}) collective-permute-start(bf16[64,2,2,128]{3,2,1,0:T(2,128)(2,1)} %get-tuple-element.362), channel_id=1, source_target_pairs={{16,0},{17,1},{18,2},{19,3},{20,4},{21,5},{22,6},{23,7},{24,8},{25... | collective-permute-start | bytes 196616 | tf_op jit(solution)/shard_map/while/body/eval_jaxpr/ppermute | solution.py:13
  20.8 1.1 collective-permute-done
  21.9 1.7 fusion.172
  23.8 0.1 fusion.175
  24.4 0.1 fusion.181
  24.6 0.2 fusion.182
  24.9 0.2 fusion.184
  25.0 0.2 fusion.185
  25.3 0.2 fusion.186
  25.4 0.2 fusion.187
  25.7 0.2 fusion.189
  26.9 0.7 reshape.81
  27.7 1.5 fusion.199
  29.2 0.6 reshape.82
  30.0 0.6 copy-done.3
  30.6 2.2 collective-permute-start
  32.8 1.1 collective-permute-done
  33.9 1.7 fusion.172
  35.8 0.1 fusion.175
  36.6 0.2 fusion.182
  36.9 0.2 fusion.184
  37.1 0.2 fusion.185
  37.3 0.2 fusion.186
  37.5 0.2 fusion.187
  37.7 0.2 fusion.189
  38.9 0.7 reshape.81
  39.7 1.5 fusion.199
  41.2 0.6 reshape.82
  42.0 0.6 copy-done.3
  42.6 0.9 reshape_squeeze.7
  43.5 2.1 fusion.130
  45.6 0.3 collective-permute-start.1
  45.9 21.8 %collective-permute-done.1 = f32[1728,64]{0,1:T(8,128)S(1)} collective-permute-done((f32[1728,64]{0,1:T(8,128)S(1)}, f32[1728,64]{0,1:T(8,128)S(1)}, u32[]{:S(2)}, u32[]{:S(2)}) %collective-permute-start.1) | collective-permute-done | bytes 442400 | tf_op jit(solution)/shard_map/ppermute | solution.py:86
  67.8 0.3 collective-permute-start.2
  68.1 10.9 %collective-permute-done.2 = f32[1728,64]{0,1:T(8,128)S(1)} collective-permute-done((f32[1728,64]{0,1:T(8,128)S(1)}, f32[1728,64]{0,1:T(8,128)S(1)}, u32[]{:S(2)}, u32[]{:S(2)}) %collective-permute-start.2) | collective-permute-done | bytes 442400 | tf_op jit(solution)/shard_map/ppermute | solution.py:86
  79.1 1.2 collective-permute-start.3
  80.3 0.6 reduce_max.19
  81.6 19.6 %collective-permute-done.3 = f32[1728,64]{0,1:T(8,128)S(1)} collective-permute-done((f32[1728,64]{0,1:T(8,128)S(1)}, f32[1728,64]{0,1:T(8,128)S(1)}, u32[]{:S(2)}, u32[]{:S(2)}) %collective-permute-start.3) | collective-permute-done | bytes 442400 | tf_op jit(solution)/shard_map/ppermute | solution.py:86
  101.3 2.3 collective-permute-start.4
  103.9 39.1 %collective-permute-done.4 = f32[1728,64]{0,1:T(8,128)S(1)} collective-permute-done((f32[1728,64]{0,1:T(8,128)S(1)}, f32[1728,64]{0,1:T(8,128)S(1)}, u32[]{:S(2)}, u32[]{:S(2)}) %collective-permute-start.4) | collective-permute-done | bytes 442400 | tf_op jit(solution)/shard_map/ppermute | solution.py:86
  142.9 0.6 fusion.61
  143.5 48.4 %all-gather.3.cloned.1.call-done = bf16[1,1728,1728]{2,0,1:T(2,128)(2,1)} async-done(((bf16[1,108,1728]{2,0,1:T(2,128)(2,1)}), bf16[1,1728,1728]{2,0,1:T(2,128)(2,1)}) %all-gather.3.cloned.1.call-update) | async-done | bytes 5971984 | tf_op jit(solution)/shard_map/all_gather | solution.py:95
  191.9 18.9 %abs_reduce_fusion = f32[1728]{0:T(1024)S(1)} fusion(bf16[1,1728,1728]{2,0,1:T(2,128)(2,1)} %all-gather.3.cloned.1.call-done), kind=kLoop, calls=%fused_computation.89 | loop fusion | flops 8956224 | bytes 5978880 | tf_op jit(solution)/shard_map/reduce_sum | solution.py:138
  210.8 0.6 reduce_max.18
  212.1 14.3 %convert_multiply_fusion = f32[1,1728,1728]{2,0,1:T(1,128)S(1)} fusion(bf16[1,1728,1728]{2,0,1:T(2,128)(2,1)} %all-gather.3.cloned.1.call-done, f32[]{:T(128)S(6)} %div.12), kind=kLoop, calls=%fused_computation.90 | loop fusion | flops 5971968 | bytes 17915908 | tf_op jit(solution)/shard_map/mul | solution.py:139
  226.5 1.3 convolution_convert_fusion.1
  227.8 1.4 fusion.55
  229.2 1.6 convolution_bitcast_fusion
  230.8 1.7 copy.18
  (86 shorter events, 7.0 us)
Async XLA Ops:
  7.2 2.7 %copy-start.4 = (bf16[1,64,1728]{2,1,0:T(8,128)(2,1)S(1)}, bf16[1,64,1728]{2,1,0:T(8,128)(2,1)}, u32[]{:S(2)}) copy-start(bf16[1,64,1728]{2,1,0:T(8,128)(2,1)} %param.11) | copy-start | bytes 663556
  7.2 4.1 %copy-start = (bf16[1,1,1,64,2,2,128]{6,5,4,3,2,1,0:T(2,128)(2,1)S(1)}, bf16[1,1,1,64,2,2,128]{6,5,4,3,2,1,0:T(2,128)(2,1)}, u32[]{:S(2)}) copy-start(bf16[1,1,1,64,2,2,128]{6,5,4,3,2,1,0:T(2,128)(2,1)} %param.8) | copy-start | bytes 196612
  7.2 184.7 %all-gather.3.cloned.1.call-start = ((), (), s32[]{:S(2)}) async-start(), calls=%async_computation | async-start | bytes 13160448 | tf_op jit(solution)/shard_map/all_gather | solution.py:95
  18.2 3.7 %collective-permute-start = (bf16[64,2,2,128]{3,2,1,0:T(2,128)(2,1)}, bf16[64,2,2,128]{3,2,1,0:T(2,128)(2,1)S(1)}, u32[]{:S(2)}, u32[]{:S(2)}) collective-permute-start(bf16[64,2,2,128]{3,2,1,0:T(2,128)(2,1)} %get-tuple-element.362), channel_id=1, source_target_pairs={{16,0},{17,1},{18,2},{19,3},{20,4},{21,5},{22,6},{23,7},{24,8},{25... | collective-permute-start | bytes 196616 | tf_op jit(solution)/shard_map/while/body/eval_jaxpr/ppermute | solution.py:13
  27.6 2.2 copy-start.2
  29.9 0.6 copy-start.3
  30.6 3.3 %collective-permute-start = (bf16[64,2,2,128]{3,2,1,0:T(2,128)(2,1)}, bf16[64,2,2,128]{3,2,1,0:T(2,128)(2,1)S(1)}, u32[]{:S(2)}, u32[]{:S(2)}) collective-permute-start(bf16[64,2,2,128]{3,2,1,0:T(2,128)(2,1)} %get-tuple-element.362), channel_id=1, source_target_pairs={{16,0},{17,1},{18,2},{19,3},{20,4},{21,5},{22,6},{23,7},{24,8},{25... | collective-permute-start | bytes 196616 | tf_op jit(solution)/shard_map/while/body/eval_jaxpr/ppermute | solution.py:13
  39.7 2.2 copy-start.2
  42.0 0.6 copy-start.3
  45.6 34.6 %copy-start.5 = (bf16[1,64,64]{2,1,0:T(8,128)(2,1)S(1)}, bf16[1,64,64]{2,1,0:T(8,128)(2,1)}, u32[]{:S(2)}) copy-start(bf16[1,64,64]{2,1,0:T(8,128)(2,1)} %param.13) | copy-start | bytes 24580
  45.6 22.1 %collective-permute-start.1 = (f32[1728,64]{0,1:T(8,128)S(1)}, f32[1728,64]{0,1:T(8,128)S(1)}, u32[]{:S(2)}, u32[]{:S(2)}) collective-permute-start(f32[1728,64]{0,1:T(8,128)S(1)} %fusion.130), channel_id=1, source_target_pairs={{0,1},{1,0},{2,3},{3,2},{4,5},{5,4},{6,7},{7,6},{8,9},{9,8},{10,11... | collective-permute-start | bytes 1327112 | tf_op jit(solution)/shard_map/ppermute | solution.py:86
  67.8 11.2 %collective-permute-start.2 = (f32[1728,64]{0,1:T(8,128)S(1)}, f32[1728,64]{0,1:T(8,128)S(1)}, u32[]{:S(2)}, u32[]{:S(2)}) collective-permute-start(f32[1728,64]{0,1:T(8,128)S(1)} %add.76), channel_id=1, source_target_pairs={{0,2},{1,3},{2,0},{3,1},{4,6},{5,7},{6,4},{7,5},{8,10},{9,11},{10,... | collective-permute-start | bytes 1327112 | tf_op jit(solution)/shard_map/ppermute | solution.py:86
  79.1 22.2 %collective-permute-start.3 = (f32[1728,64]{0,1:T(8,128)S(1)}, f32[1728,64]{0,1:T(8,128)S(1)}, u32[]{:S(2)}, u32[]{:S(2)}) collective-permute-start(f32[1728,64]{0,1:T(8,128)S(1)} %add.77), channel_id=1, source_target_pairs={{0,4},{1,5},{2,6},{3,7},{4,0},{5,1},{6,2},{7,3},{8,12},{9,13},{10,... | collective-permute-start | bytes 1327112 | tf_op jit(solution)/shard_map/ppermute | solution.py:86
  101.3 41.6 %collective-permute-start.4 = (f32[1728,64]{0,1:T(8,128)S(1)}, f32[1728,64]{0,1:T(8,128)S(1)}, u32[]{:S(2)}, u32[]{:S(2)}) collective-permute-start(f32[1728,64]{0,1:T(8,128)S(1)} %add.78), channel_id=1, source_target_pairs={{0,8},{1,9},{2,10},{3,11},{4,12},{5,13},{6,14},{7,15},{8,0},{9,1},... | collective-permute-start | bytes 1327112 | tf_op jit(solution)/shard_map/ppermute | solution.py:86
  212.1 14.3 %copy-start.1 = (bf16[1,108,1728]{2,1,0:T(8,128)(2,1)S(1)}, bf16[1,108,1728]{2,1,0:T(8,128)(2,1)}, u32[]{:S(2)}) copy-start(bf16[1,108,1728]{2,1,0:T(8,128)(2,1)} %param.12) | copy-start | bytes 1119748
Sparse Core Ops, SparseCore 0:
  11.4 180.4 all-gather.2
where the time goes:
time: 240 us; the launch traced here: 239 us
  waiting for transfers between devices  142 us (59%)
  other arithmetic  38.3 us (16%)
  local copies, waits for them, and re-layouts  24.1 us (10%)
  between operations  15.6 us (6%)
  matrix products  10.2 us (4%)
  starting transfers between devices  8.92 us (4%)
    ppermute x4, waiting for transfers between devices, doubling_sum(): lax.ppermute(value, axis, [(i, i ^ stride) for i in range(count)])  91.4 us
    all_gather x1, waiting for transfers between devices, shards(): gathered = lax.all_gather(a_factor[0], 'dp', axis=0, tiled=True)  48.4 us
    reduce_sum x1, other arithmetic, shards(): step_size = 1.0 / jnp.max(jnp.sum(jnp.abs(full_values), axis=1))  18.9 us
    mul x1, other arithmetic, shards(): step_size * full_values  14.3 us
    unnamed x37, local copies, waits for them, and re-layouts  8.38 us
    while x60, local copies, waits for them, and re-layouts  7.65 us
    ppermute x2, starting transfers between devices, shifted(): lax.ppermute(value, axis, [(source, source + steps) for source in range(f...  4.81 us
  transfers between devices with their start and end apart: 7, of which 7 were waited for; matrix products, arithmetic and copies ran while one was open for 12% of the time, Pallas kernels for 0%

commit v1 on v0

--- a/solution.py
+++ b/solution.py
@@ -92,7 +92,14 @@
     section_index = lax.axis_index("section")
     section_count = lax.axis_size("section")
     tick_count = MICRO + section_count - 1
-    gathered = lax.all_gather(a_factor[0], "dp", axis=0, tiled=True)
+    ways, here = (lax.axis_size("dp"), lax.axis_index("dp"))
+    gathered, reach = (a_factor[0], 1)
+    while reach < ways:
+        theirs = lax.ppermute(gathered, "dp", [(d, d ^ reach) for d in range(ways)])
+        mine_first = jnp.concatenate([gathered, theirs], axis=0)
+        theirs_first = jnp.concatenate([theirs, gathered], axis=0)
+        gathered = jnp.where(here & reach == 0, mine_first, theirs_first)
+        reach = 2 * reach
     inputs = acts[0, 0]
     pre_values = preacts[0, 0]
     upper_grads = top_grad[0]

time: 240 us -> 290 us (1.21)
  local copies, waits for them, and re-layouts: 24.1 us -> 75 us
  other arithmetic: 38.3 us -> 16.4 us
  waiting for transfers between devices: 142 us -> 162 us
  between operations: 15.6 us -> 2.2 us
  matrix products: 10.2 us -> 20.2 us
  starting transfers between devices: 8.92 us -> 12.9 us
    ppermute x4, waiting for transfers between devices: 91.4 us -> 141 us  [doubling_sum(): lax.ppermute(value, axis, [(i, i ^ stride) for i in range(count)])]
    all_gather x1 -> x0, waiting for transfers between devices: 48.4 us -> none  [shards(): gathered = lax.all_gather(a_factor[0], 'dp', axis=0, tiled=True)]
    while x60 -> x52, local copies, waits for them, and re-layouts: 7.65 us -> 37.6 us
    ppermute x0 -> x4, waiting for transfers between devices: none -> 19.2 us  [shards(): theirs = lax.ppermute(gathered, 'dp', [(d, d ^ reach) for d in range(ways)])]
    mul x1 -> x0, other arithmetic: 14.3 us -> none  [shards(): step_size * full_values]
    unnamed x37 -> x40, local copies, waits for them, and re-layouts: 8.38 us -> 20.8 us
    reduce_sum x1, other arithmetic: 18.9 us -> 7.51 us  [shards(): step_size = 1.0 / jnp.max(jnp.sum(jnp.abs(full_values), axis=1))]
    reshape x3, local copies, waits for them, and re-layouts: 3.71 us -> 12.8 us  [taps_stack(): stacked.reshape(len(pieces) * volume.shape[0], size_x * size_y * size_z)]
  transfers between devices with their start and end apart: 7 -> 10, of which waited for: 7 -> 8; matrix products, arithmetic and copies ran while one was open for 12% -> 27% of each run, Pallas kernels for 0% -> 0%
where the time goes in v1:
time: 290 us; the launch traced here: 289 us
  waiting for transfers between devices  162 us (56%)
  local copies, waits for them, and re-layouts  75 us (26%)
  matrix products  20.2 us (7%)
  other arithmetic  16.4 us (6%)
  starting transfers between devices  12.9 us (4%)
    ppermute x4, waiting for transfers between devices, doubling_sum(): lax.ppermute(value, axis, [(i, i ^ stride) for i in range(count)])  141 us
    while x52, local copies, waits for them, and re-layouts  37.6 us
    unnamed x40, local copies, waits for them, and re-layouts  20.8 us
    ppermute x4, waiting for transfers between devices, shards(): theirs = lax.ppermute(gathered, 'dp', [(d, d ^ reach) for d in range(ways)])  19.2 us
    reshape x3, local copies, waits for them, and re-layouts, taps_stack(): stacked.reshape(len(pieces) * volume.shape[0], size_x * size_y * size_z)  12.8 us
    dot_general x1, matrix products, shards(): jnp.dot(resid0, full_resid0, preferred_element_type=jnp.float32)  8.14 us
    dot_general x1, matrix products, shards(): jnp.dot(resid1, full_resid0, preferred_element_type=jnp.float32)  7.77 us
    reduce_sum x1, other arithmetic, shards(): step_size = 1.0 / jnp.max(jnp.sum(jnp.abs(full_values), axis=1))  7.51 us
  transfers between devices with their start and end apart: 10, of which 8 were waited for; matrix products, arithmetic and copies ran while one was open for 27% of the time, Pallas kernels for 0%

profile of v1, /device:TPU:7, one launch (start us, length us, event | category | flops | bytes accessed | tf_op | source)
XLA Modules:
  0.0 288.7 jit_solution(12008571441866292264)
XLA Ops:
  1.0 1.4 reshape_squeeze.6
  2.6 0.7 fusion.75
  4.0 7.1 %collective-permute-done.1 = bf16[108,1728]{1,0:T(8,128)(2,1)S(1)} collective-permute-done((bf16[108,1728]{1,0:T(8,128)(2,1)}, bf16[108,1728]{1,0:T(8,128)(2,1)S(1)}, u32[]{:S(2)}, u32[]{:S(2)}) %collective-permute-start.1) | collective-permute-done | bytes 373280 | tf_op jit(solution)/shard_map/ppermute | solution.py:98
  11.7 0.7 fusion.79
  12.4 0.7 fusion.81
  15.9 0.7 fusion.91
  16.7 12.1 %collective-permute-done.2 = bf16[216,1728]{1,0:T(8,128)(2,1)S(1)} collective-permute-done((bf16[216,1728]{1,0:T(8,128)(2,1)S(1)}, bf16[216,1728]{1,0:T(8,128)(2,1)S(1)}, u32[]{:S(2)}, u32[]{:S(2)}) %collective-permute-start.2) | collective-permute-done | bytes 746528 | tf_op jit(solution)/shard_map/ppermute | solution.py:98
  28.7 1.6 maximum_select_fusion.2
  30.4 1.3 collective-permute-start.3
  31.8 58.1 %while.20 = (s32[]{:T(128)}, bf16[64,2,2,128]{3,2,1,0:T(2,128)(2,1)S(1)}, bf16[1,64,2,2,128]{4,3,2,1,0:T(2,128)(2,1)S(1)}, bf16[1,64,2,2,128]{4,3,2,1,0:T(2,128)...) while((s32[]{:T(128)}, ...), condition=%wide.region_1.2_spmd.clone, body=%wide.region_0.1_spmd.clone.sunk | while | flops 113475592 | bytes 10248395 | solution.py:136
  32.0 4.6 %collective-permute-start = (bf16[64,2,2,128]{3,2,1,0:T(2,128)(2,1)S(1)}, bf16[64,2,2,128]{3,2,1,0:T(2,128)(2,1)S(1)}, u32[]{:S(2)}, u32[]{:S(2)}) collective-permute-start(bf16[64,2,2,128]{3,2,1,0:T(2,128)(2,1)S(1)} %get-tuple-element.350), channel_id=1, source_target_pairs={{16,0},{17,1},{18,2},{19,3},{20,4},{21,5},{22,6},{23,7},{24,8},{25... | collective-permute-start | bytes 196616 | tf_op jit(solution)/shard_map/while/body/eval_jaxpr/ppermute | solution.py:13
  36.6 0.9 collective-permute-done
  37.6 0.7 fusion.183
  39.0 0.7 fusion.185
  41.9 0.7 fusion.189
  43.3 0.7 fusion.191
  44.0 0.8 fusion.192
  45.5 0.8 fusion.194
  46.3 0.8 fusion.195
  47.7 0.8 fusion.196
  48.5 0.8 fusion.197
  50.0 0.8 fusion.199
  52.2 0.7 fusion.202
  56.4 0.7 fusion.208
  57.2 4.3 %reshape.73 = bf16[1728,512]{1,0:T(8,128)(2,1)S(1)} reshape(bf16[27,64,2,2,128]{4,3,2,1,0:T(2,128)(2,1)} %fusion.208) | data formatting | bytes 3538944 | tf_op jit(solution)/shard_map/while/body/eval_jaxpr/reshape | solution.py:44
  62.1 2.3 collective-permute-start
  64.4 0.9 collective-permute-done
  65.4 0.7 fusion.183
  66.8 0.7 fusion.185
  69.7 0.7 fusion.189
  71.1 0.7 fusion.191
  71.8 0.8 fusion.192
  73.3 0.8 fusion.194
  74.1 0.8 fusion.195
  75.5 0.8 fusion.196
  76.3 0.8 fusion.197
  77.8 0.8 fusion.199
  78.6 0.7 fusion.200
  80.0 0.7 fusion.202
  84.2 0.7 fusion.208
  85.0 4.3 %reshape.73 = bf16[1728,512]{1,0:T(8,128)(2,1)S(1)} reshape(bf16[27,64,2,2,128]{4,3,2,1,0:T(2,128)(2,1)} %fusion.208) | data formatting | bytes 3538944 | tf_op jit(solution)/shard_map/while/body/eval_jaxpr/reshape | solution.py:44
  89.9 0.8 fusion.93
  91.4 0.8 fusion.97
  92.2 0.8 fusion.99
  93.7 0.8 fusion.101
  94.4 0.8 fusion.103
  95.9 0.8 fusion.107
  96.7 0.7 fusion.109
  98.1 0.7 fusion.113
  98.9 4.6 %maximum_select_fusion.1 = bf16[864,1728]{1,0:T(8,128)(2,1)} fusion(bf16[432,1728]{1,0:T(8,128)(2,1)} %collective-permute-done.3, bf16[432,1728]{1,0:T(8,128)(2,1)} %maximum_select_fusion.2, pred[]{:T(512)S(6)} %eq.44), kind=kLoop, calls=%fused_computation.122 | loop fusion | flops 13436928 | bytes 5971969 | tf_op jit(solution)/shard_map/jit(_where)/select_n | solution.py:101
  103.5 2.3 collective-permute-start.4
  107.9 0.7 fusion.121
  109.3 0.7 fusion.125
  110.1 4.3 %reshape.66 = bf16[1728,512]{1,0:T(8,128)(2,1)S(1)} reshape(bf16[27,64,2,2,128]{4,3,2,1,0:T(2,128)(2,1)} %fusion.125) | data formatting | bytes 3538944 | tf_op jit(solution)/shard_map/reshape | solution.py:44
  115.4 11.3 %collective-permute-done.5 = f32[1728,64]{0,1:T(8,128)S(1)} collective-permute-done((f32[1728,64]{0,1:T(8,128)S(1)}, f32[1728,64]{0,1:T(8,128)S(1)}, u32[]{:S(2)}, u32[]{:S(2)}) %collective-permute-start.5) | collective-permute-done | bytes 442400 | tf_op jit(solution)/shard_map/ppermute | solution.py:86
  127.0 10.6 %collective-permute-done.6 = f32[1728,64]{0,1:T(8,128)S(1)} collective-permute-done((f32[1728,64]{0,1:T(8,128)S(1)}, f32[1728,64]{0,1:T(8,128)S(1)}, u32[]{:S(2)}, u32[]{:S(2)}) %collective-permute-start.6) | collective-permute-done | bytes 442400 | tf_op jit(solution)/shard_map/ppermute | solution.py:86
  139.3 42.7 %collective-permute-done.7 = f32[1728,64]{0,1:T(8,128)S(1)} collective-permute-done((f32[1728,64]{0,1:T(8,128)S(1)}, f32[1728,64]{0,1:T(8,128)S(1)}, u32[]{:S(2)}, u32[]{:S(2)}) %collective-permute-start.7) | collective-permute-done | bytes 442400 | tf_op jit(solution)/shard_map/ppermute | solution.py:86
  182.0 1.0 collective-permute-start.8
  183.3 76.2 %collective-permute-done.8 = f32[1728,64]{0,1:T(8,128)S(1)} collective-permute-done((f32[1728,64]{0,1:T(8,128)S(1)}, f32[1728,64]{0,1:T(8,128)S(1)}, u32[]{:S(2)}, u32[]{:S(2)}) %collective-permute-start.8) | collective-permute-done | bytes 442400 | tf_op jit(solution)/shard_map/ppermute | solution.py:86
  260.1 7.5 %fusion.54 = f32[1728]{0:T(1024)S(1)} fusion(bf16[864,1728]{1,0:T(8,128)(2,1)} %maximum_select_fusion.1, bf16[864,1728]{1,0:T(8,128)(2,1)} %collective-permute-done.4, pred[]{:T(512)S(6)} %eq.43), kind=kLoop, calls=%fused_computation.89 | loop fusion | flops 35830080 | bytes 5978881 | tf_op jit(solution)/shard_map/reduce_sum | solution.py:145
  268.9 8.1 %fusion.61 = bf16[108,1728]{1,0:T(8,128)(2,1)S(1)} fusion(f32[]{:T(128)S(6)} %div.12, s32[108]{0:T(128)S(1)} %iota_add_fusion, bf16[1,108,1728]{2,1,0:T(8,128)(2,1)S(1)} %copy-done.1, bf16[864,1728]{1,0:T(8,128)(2,1)} %collective-permute-done.4, bf16[864,1728]{1,0:T(8,128)(2,1)} %maximum_select_fusion.1, pred[]{:T(512)S(6)} %eq.43), kind=kOutput, calls=%fused_computation.123 | convolution fusion | flops 691068672 | bytes 6718901 | tf_op jit(solution)/shard_map/dot_general | solution.py:151
  277.0 7.8 %fusion.57 = f32[108,1728]{1,0:T(8,128)S(1)} fusion(bf16[108,1728]{1,0:T(8,128)(2,1)S(1)} %fusion.61, f32[]{:T(128)S(6)} %div.12, bf16[864,1728]{1,0:T(8,128)(2,1)} %collective-permute-done.4, bf16[864,1728]{1,0:T(8,128)(2,1)} %maximum_select_fusion.1, pred[]{:T(512)S(6)} %eq.43), kind=kOutput, calls=%fused_computation.94 | convolution fusion | flops 689762304 | bytes 7091717 | tf_op jit(solution)/shard_map/dot_general | solution.py:152
  285.2 1.9 convolution_bitcast_fusion
  287.0 1.7 copy.14
  (89 shorter events, 36.1 us)
Async XLA Ops:
  0.6 10.5 %copy-start.1 = (bf16[1,108,1728]{2,1,0:T(8,128)(2,1)S(1)}, bf16[1,108,1728]{2,1,0:T(8,128)(2,1)}, u32[]{:S(2)}) copy-start(bf16[1,108,1728]{2,1,0:T(8,128)(2,1)} %param.12) | copy-start | bytes 1119748
  0.6 1.9 copy-start
  0.6 10.5 %collective-permute-start.1 = (bf16[108,1728]{1,0:T(8,128)(2,1)}, bf16[108,1728]{1,0:T(8,128)(2,1)S(1)}, u32[]{:S(2)}, u32[]{:S(2)}) collective-permute-start(bf16[108,1728]{1,0:T(8,128)(2,1)} %bitcast.355), channel_id=1, source_target_pairs={{0,1},{1,0},{2,3},{3,2},{4,5},{5,4},{6,7},{7,6},{8,9},{9,8},{10,11... | collective-permute-start | bytes 1119752 | tf_op jit(solution)/shard_map/ppermute | solution.py:98
  11.4 17.4 %collective-permute-start.2 = (bf16[216,1728]{1,0:T(8,128)(2,1)S(1)}, bf16[216,1728]{1,0:T(8,128)(2,1)S(1)}, u32[]{:S(2)}, u32[]{:S(2)}) collective-permute-start(bf16[216,1728]{1,0:T(8,128)(2,1)S(1)} %maximum_select_fusion.3), channel_id=1, source_target_pairs={{0,2},{1,3},{2,0},{3,1},{4,6},{5,7},{6,4},{7,5},{8,10},{9,11},{10,... | collective-permute-start | bytes 2239496 | tf_op jit(solution)/shard_map/ppermute | solution.py:98
  15.3 16.5 %copy-start.3 = (bf16[1,1,1,64,2,2,128]{6,5,4,3,2,1,0:T(2,128)(2,1)S(1)}, bf16[1,1,1,64,2,2,128]{6,5,4,3,2,1,0:T(2,128)(2,1)}, u32[]{:S(2)}) copy-start(bf16[1,1,1,64,2,2,128]{6,5,4,3,2,1,0:T(2,128)(2,1)} %param.9) | copy-start | bytes 196612
  15.3 16.5 %copy-start.4 = (bf16[1,1,64,2,2,128]{5,4,3,2,1,0:T(2,128)(2,1)S(1)}, bf16[1,1,64,2,2,128]{5,4,3,2,1,0:T(2,128)(2,1)}, u32[]{:S(2)}) copy-start(bf16[1,1,64,2,2,128]{5,4,3,2,1,0:T(2,128)(2,1)} %param.10) | copy-start | bytes 196612
  30.4 68.5 %collective-permute-start.3 = (bf16[432,1728]{1,0:T(8,128)(2,1)}, bf16[432,1728]{1,0:T(8,128)(2,1)}, u32[]{:S(2)}, u32[]{:S(2)}) collective-permute-start(bf16[432,1728]{1,0:T(8,128)(2,1)} %maximum_select_fusion.2), channel_id=1, source_target_pairs={{0,4},{1,5},{2,6},{3,7},{4,0},{5,1},{6,2},{7,3},{8,12},{9,13},{10,... | collective-permute-start | bytes 4478984 | tf_op jit(solution)/shard_map/ppermute | solution.py:98
  32.0 5.5 %collective-permute-start = (bf16[64,2,2,128]{3,2,1,0:T(2,128)(2,1)S(1)}, bf16[64,2,2,128]{3,2,1,0:T(2,128)(2,1)S(1)}, u32[]{:S(2)}, u32[]{:S(2)}) collective-permute-start(bf16[64,2,2,128]{3,2,1,0:T(2,128)(2,1)S(1)} %get-tuple-element.350), channel_id=1, source_target_pairs={{16,0},{17,1},{18,2},{19,3},{20,4},{21,5},{22,6},{23,7},{24,8},{25... | collective-permute-start | bytes 196616 | tf_op jit(solution)/shard_map/while/body/eval_jaxpr/ppermute | solution.py:13
  62.1 3.1 %collective-permute-start = (bf16[64,2,2,128]{3,2,1,0:T(2,128)(2,1)S(1)}, bf16[64,2,2,128]{3,2,1,0:T(2,128)(2,1)S(1)}, u32[]{:S(2)}, u32[]{:S(2)}) collective-permute-start(bf16[64,2,2,128]{3,2,1,0:T(2,128)(2,1)S(1)} %get-tuple-element.350), channel_id=1, source_target_pairs={{16,0},{17,1},{18,2},{19,3},{20,4},{21,5},{22,6},{23,7},{24,8},{25... | collective-permute-start | bytes 196616 | tf_op jit(solution)/shard_map/while/body/eval_jaxpr/ppermute | solution.py:13
  89.9 13.6 %copy-start.2 = (bf16[1,64,2,2,128]{4,3,2,1,0:T(2,128)(2,1)}, bf16[1,64,2,2,128]{4,3,2,1,0:T(2,128)(2,1)S(1)}, u32[]{:S(2)}) copy-start(bf16[1,64,2,2,128]{4,3,2,1,0:T(2,128)(2,1)S(1)} %get-tuple-element.209) | copy-start | bytes 196612
  103.5 156.6 %collective-permute-start.4 = (bf16[864,1728]{1,0:T(8,128)(2,1)}, bf16[864,1728]{1,0:T(8,128)(2,1)}, u32[]{:S(2)}, u32[]{:S(2)}) collective-permute-start(bf16[864,1728]{1,0:T(8,128)(2,1)} %maximum_select_fusion.1), channel_id=1, source_target_pairs={{0,8},{1,9},{2,10},{3,11},{4,12},{5,13},{6,14},{7,15},{8,0},{9,1},... | collective-permute-start | bytes 8957960 | tf_op jit(solution)/shard_map/ppermute | solution.py:98
  115.0 22.8 %copy-start.5 = (bf16[1,64,64]{2,1,0:T(8,128)(2,1)S(1)}, bf16[1,64,64]{2,1,0:T(8,128)(2,1)}, u32[]{:S(2)}) copy-start(bf16[1,64,64]{2,1,0:T(8,128)(2,1)} %param.13) | copy-start | bytes 24580
  115.0 11.6 %collective-permute-start.5 = (f32[1728,64]{0,1:T(8,128)S(1)}, f32[1728,64]{0,1:T(8,128)S(1)}, u32[]{:S(2)}, u32[]{:S(2)}) collective-permute-start(f32[1728,64]{0,1:T(8,128)S(1)} %fusion.141), channel_id=1, source_target_pairs={{0,1},{1,0},{2,3},{3,2},{4,5},{5,4},{6,7},{7,6},{8,9},{9,8},{10,11... | collective-permute-start | bytes 1327112 | tf_op jit(solution)/shard_map/ppermute | solution.py:86
  126.7 10.9 %collective-permute-start.6 = (f32[1728,64]{0,1:T(8,128)S(1)}, f32[1728,64]{0,1:T(8,128)S(1)}, u32[]{:S(2)}, u32[]{:S(2)}) collective-permute-start(f32[1728,64]{0,1:T(8,128)S(1)} %add.76), channel_id=1, source_target_pairs={{0,2},{1,3},{2,0},{3,1},{4,6},{5,7},{6,4},{7,5},{8,10},{9,11},{10,... | collective-permute-start | bytes 1327112 | tf_op jit(solution)/shard_map/ppermute | solution.py:86
  137.6 44.3 %collective-permute-start.7 = (f32[1728,64]{0,1:T(8,128)S(1)}, f32[1728,64]{0,1:T(8,128)S(1)}, u32[]{:S(2)}, u32[]{:S(2)}) collective-permute-start(f32[1728,64]{0,1:T(8,128)S(1)} %add.77), channel_id=1, source_target_pairs={{0,4},{1,5},{2,6},{3,7},{4,0},{5,1},{6,2},{7,3},{8,12},{9,13},{10,... | collective-permute-start | bytes 1327112 | tf_op jit(solution)/shard_map/ppermute | solution.py:86
  182.0 77.5 %collective-permute-start.8 = (f32[1728,64]{0,1:T(8,128)S(1)}, f32[1728,64]{0,1:T(8,128)S(1)}, u32[]{:S(2)}, u32[]{:S(2)}) collective-permute-start(f32[1728,64]{0,1:T(8,128)S(1)} %add.78), channel_id=1, source_target_pairs={{0,8},{1,9},{2,10},{3,11},{4,12},{5,13},{6,14},{7,15},{8,0},{9,1},... | collective-permute-start | bytes 1327112 | tf_op jit(solution)/shard_map/ppermute | solution.py:86
